TPU v7x, 256 devices: a whole 4x4x8 slice. The times are simulated.
256 devices in a mesh: head: 8 (over z), vocab: 32 (over y, x, core).
Axes of the slice: x: 4, y: 4, z: 8, core: 2. Of those that a mesh axis runs over, the one named last changes fastest.
Arguments:
- hidden_states: bfloat16 [2048, 8192], P(('head', 'vocab')), may hold values from -6 to 6
- head_weight: bfloat16 [8, 8192, 16384], P('head', None, 'vocab'), may hold values from -1 to 1
- tags: int32 [2048, 1], P(('head', 'vocab')), may hold values from 0 to 7; in each aligned block of 8 rows (0 to 7, 8 to 15, ...) at most 2 rows name the same one
- targets: int32 [2048], P(('head', 'vocab')), may hold values from 0 to 16383
- row_grad: bfloat16 [2048], P(('head', 'vocab')), may hold values from -192 to 192
Outputs:
- row_loss: bfloat16 [2048], P(('head', 'vocab'))
- hidden_grad: bfloat16 [2048, 8192], P(('head', 'vocab'))
Inputs may be any that keep to these rules, and one draw needn't show every extreme that they name: `tags`: in each aligned block of 8 rows (the rows of one device) no head is named by more than 2 rows, and in every draw some block has exactly 2 rows of one head.
All inputs are finite; a program needn't handle non-finite values.
Results may differ from a plain program's by a relative error of at most 0.018.
Values may be sent and summed in bfloat16 or wider, within the bound.
No kernel may reach another device: no remote copies, remote signals or barrier semaphores. Data moves between devices by JAX's collectives and lax.ppermute only.
A program may use at most 64 MiB of HBM per device.

v0:
```python
import jax
import jax.numpy as jnp
from jax import lax
from jax.sharding import PartitionSpec as P

CAP = 2


def project_back(dlog_block, weight):
    return lax.dot_general(
        dlog_block, weight, (((1,), (1,)), ((), ())), preferred_element_type=jnp.float32
    )


def per_device(hidden_states, head_weight, tags, targets, row_grad):
    head_count = lax.axis_size("head")
    own_rows = head_count * CAP
    row_tag = tags[:, 0]
    local_rows = row_tag.shape[0]
    row_iota = lax.broadcasted_iota(jnp.int32, (local_rows, local_rows), 0)
    col_iota = lax.broadcasted_iota(jnp.int32, (local_rows, local_rows), 1)
    earlier = (row_tag[None, :] == row_tag[:, None]) & (col_iota < row_iota)
    slot_rank = jnp.sum(earlier.astype(jnp.int32), axis=1)
    slot_index = row_tag * CAP + slot_rank
    selector = jnp.arange(own_rows, dtype=jnp.int32)[:, None] == slot_index[None, :]
    send_rows = jnp.dot(
        selector.astype(jnp.bfloat16), hidden_states, preferred_element_type=jnp.float32
    ).astype(jnp.bfloat16)
    send_rows = send_rows.reshape(head_count, CAP, hidden_states.shape[1])
    send_targets = jnp.sum(jnp.where(selector, targets[None, :], 0), axis=1).reshape(
        head_count, CAP
    )
    send_scale = (
        jnp.sum(jnp.where(selector, row_grad[None, :].astype(jnp.float32), 0.0), axis=1)
        .astype(jnp.bfloat16)
        .reshape(head_count, CAP)
    )
    arrived = (
        lax.all_to_all(send_rows, "head", split_axis=0, concat_axis=0, tiled=True),
        lax.all_to_all(send_targets, "head", split_axis=0, concat_axis=0, tiled=True),
        lax.all_to_all(send_scale, "head", split_axis=0, concat_axis=0, tiled=True),
    )
    grouped = (
        lax.all_gather(arrived[0], "vocab", axis=0, tiled=True),
        lax.all_gather(arrived[1], "vocab", axis=0, tiled=True),
        lax.all_gather(arrived[2], "vocab", axis=0, tiled=True),
    )
    gathered = grouped[0].reshape(-1, hidden_states.shape[1])
    group_targets = grouped[1].reshape(-1)
    group_scale = grouped[2].reshape(-1).astype(jnp.float32)
    weight = head_weight[0]
    vocab_width = weight.shape[1]
    logits = jnp.dot(gathered, weight, preferred_element_type=jnp.float32)
    offset = lax.axis_index("vocab") * vocab_width
    target_hit = lax.broadcasted_iota(jnp.int32, logits.shape, 1) + offset == group_targets[:, None]
    own_target = jnp.sum(jnp.where(target_hit, logits, 0.0), axis=1)
    row_top = lax.pmax(jnp.max(logits, axis=1), "vocab")
    local_total = jnp.sum(jnp.exp(logits - row_top[:, None]), axis=1)
    row_total, target_logit = lax.psum((local_total, own_target), "vocab")
    group_loss = (jnp.log(row_total) + row_top - target_logit).astype(jnp.bfloat16)
    probabilities = jnp.exp(logits - row_top[:, None]) / row_total[:, None]
    dlogits = (group_scale[:, None] * (probabilities - target_hit.astype(jnp.float32))).astype(
        jnp.bfloat16
    )
    partial_value = project_back(dlogits, weight)
    summed = lax.psum(partial_value.astype(jnp.bfloat16), "vocab").astype(jnp.float32)
    own_grad = lax.dynamic_slice_in_dim(summed, lax.axis_index("vocab") * own_rows, own_rows, 0)
    own_loss = lax.dynamic_slice_in_dim(group_loss, lax.axis_index("vocab") * own_rows, own_rows, 0)
    returned = (
        lax.all_to_all(
            own_grad.astype(jnp.bfloat16).reshape(head_count, CAP, -1),
            "head",
            split_axis=0,
            concat_axis=0,
            tiled=True,
        ),
        lax.all_to_all(
            own_loss.reshape(head_count, CAP), "head", split_axis=0, concat_axis=0, tiled=True
        ),
    )
    back_grad = returned[0].reshape(own_rows, -1)
    back_loss = returned[1].reshape(1, own_rows).astype(jnp.float32)
    hidden_grad = jnp.dot(
        selector.T.astype(jnp.bfloat16), back_grad, preferred_element_type=jnp.float32
    ).astype(jnp.bfloat16)
    row_loss = jnp.sum(jnp.where(selector.T, back_loss, 0.0), axis=1).astype(jnp.bfloat16)
    return (row_loss, hidden_grad)


def solution(mesh):
    placed = (
        P(("head", "vocab"), None),
        P("head", None, "vocab"),
        P(("head", "vocab"), None),
        P(("head", "vocab")),
        P(("head", "vocab")),
    )
    return jax.shard_map(
        per_device,
        mesh=mesh,
        in_specs=placed,
        out_specs=(P(("head", "vocab")), P(("head", "vocab"), None)),
        check_vma=False,
    )
```

profile of v0, /device:TPU:2, one launch (start us, length us, event | category | flops | bytes accessed | tf_op | source)
XLA Modules:
  0.0 414.5 jit_solution(14301299727951055076)
XLA Ops:
  7.2 0.0 copy-start
  7.2 0.0 all-gather.4.cloned.1.call-start
  7.2 0.9 convert_reduce_fusion.2
  8.1 0.7 multiply_add_fusion
  8.8 0.0 copy-done
  8.8 0.3 convolution_convert_fusion.1
  9.1 0.2 reshape.73
  9.3 20.2 %all_to_all.41 = bf16[8,2,8192]{2,1,0:T(2,128)(2,1)} all-to-all(bf16[8,2,8192]{2,1,0:T(2,128)(2,1)S(1)} %reshape.73), channel_id=1, replica_groups=mesh['head'=8,'vocab'=32] {'head'}, dimensions={0} | all-to-all | bytes 524288 | tf_op jit(solution)/shard_map/all_to_all | solution.py:39
  29.6 0.0 all-gather.4.cloned.1.call-update
  29.6 0.7 convert_element_type.77
  30.3 0.1 select_reduce_fusion
  30.4 0.7 convert_element_type.91
  31.0 3.3 all-to-all-start.3
  34.3 0.7 select_reduce_fusion.2
  35.1 0.7 all_to_all.27
  35.8 6.2 %all-to-all-done.3 = bf16[8,1,2]{2,1,0:T(2,128)(2,1)S(1)} async-done(((bf16[8,1,2]{2,1,0:T(2,128)(2,1)}), bf16[8,1,2]{2,1,0:T(2,128)(2,1)S(1)}, u32[]{:S(2)}, u32[]{:S(2)}) %all-to-all-start.3) | async-done | bytes 64 | tf_op jit(solution)/shard_map/all_to_all | solution.py:41
  41.9 3.3 all-to-all-start.1
  45.3 0.0 all-reduce.3.cloned.1.call-start
  45.3 25.0 %all-gather.1 = bf16[256,1,2]{2,1,0:T(2,128)(2,1)S(1)} all-gather(bf16[8,1,2]{2,1,0:T(2,128)(2,1)S(1)} %all-to-all-done.3), channel_id=3, replica_groups=mesh['head'=8,'vocab'=32] {'vocab'}, dimensions={0}, use_global_device_ids=true | all-gather | bytes 1056 | tf_op jit(solution)/shard_map/all_gather | solution.py:46
  70.3 0.4 convert_reduce_fusion
  70.6 0.1 reshape.78
  70.8 0.0 all-to-all-done.1
  70.8 22.7 %all-gather = s32[256,1,2]{2,1,0:T(1,128)S(1)} all-gather(s32[8,1,2]{2,1,0:T(1,128)S(1)} %all-to-all-done.1), channel_id=2, replica_groups=mesh['head'=8,'vocab'=32] {'vocab'}, dimensions={0}, use_global_device_ids=true | all-gather | bytes 2112 | tf_op jit(solution)/shard_map/all_gather | solution.py:45
  93.5 0.5 broadcast.26
  94.0 1.0 reduce.11
  95.0 0.1 eq.52
  95.1 0.0 all-gather.4.cloned.1.call-done
  95.1 13.1 %reshape.74 = bf16[512,8192]{1,0:T(8,128)(2,1)} reshape(bf16[256,2,8192]{2,1,0:T(2,128)(2,1)} %all-gather.4.cloned.1.call-done) | data formatting | bytes 16777216 | tf_op jit(solution)/shard_map/reshape | solution.py:48
  108.2 11.0 %fusion.17 = (f32[512]{0:T(512)S(1)}, f32[512,512]{0,1:T(8,128)S(1)}) fusion(bf16[512,8192]{1,0:T(8,128)(2,1)} %reshape.74, bf16[1,8192,512]{2,1,0:T(8,128)(2,1)} %param.6), kind=kOutput, calls=%fused_computation.35 | convolution fusion | flops 4295228928 | bytes 17827840 | tf_op jit(solution)/shard_map/dot_general | solution.py:53
  119.3 62.0 %pmax.7 = f32[512]{0:T(512)S(1)} all-reduce(f32[512]{0:T(512)S(1)} %get-tuple-element.6), channel_id=1, replica_groups=mesh['head'=8,'vocab'=32] {'vocab'}, use_global_device_ids=true, to_apply=%region_2.3 | all-reduce | flops 512 | bytes 4096 | tf_op jit(solution)/shard_map/pmax | solution.py:57
  181.2 0.3 fusion.7
  181.5 62.7 %all-reduce = (f32[512]{0:T(512)S(1)}, f32[512]{0:T(512)S(1)}) all-reduce(f32[512]{0:T(512)S(1)} %get-tuple-element.3, f32[512]{0:T(512)S(1)} %get-tuple-element.2), channel_id=1, replica_groups=mesh['head'=8,'vocab'=32] {'vocab'}, use_global_device_ids=true, to_apply=%region_7.8 | all-reduce | flops 1024 | bytes 8192 | tf_op jit(solution)/shard_map/psum | solution.py:59
  244.2 10.4 %convolution_convert_fusion = bf16[512,8192]{1,0:T(8,128)(2,1)} fusion(bf16[1,8192,512]{2,1,0:T(8,128)(2,1)} %param.6, f32[512,512]{0,1:T(8,128)S(1)} %get-tuple-element.7, f32[512]{0:T(512)S(1)} %get-tuple-element.5, f32[512]{0:T(512)S(1)} %reshape.78, s32[512]{0:T(512)S(1)} %eq.52, f32[512]{0:T(512)S(1)} %pmax.7, s32[512]{0:T(512)S(1)} %iota_add_fusion), kind=kOutput, calls=%fused_computation | convolution fusion | flops 4300996608 | bytes 17836032 | tf_op jit(solution)/shard_map/dot_general | solution.py:10
  254.6 0.0 all-reduce.3.cloned.1.call-update
  254.7 0.1 dynamic_slice.6
  254.7 0.7 all_to_all.35
  255.4 7.0 %all-to-all-start.2 = ((bf16[8,1,2]{2,1,0:T(2,128)(2,1)}), bf16[8,1,2]{2,1,0:T(2,128)(2,1)S(1)}, u32[]{:S(2)}, u32[]{:S(2)}) async-start(bf16[8,1,2]{2,1,0:T(2,128)(2,1)} %all_to_all.35), calls=%async_computation.2 | async-start | bytes 8192 | tf_op jit(solution)/shard_map/all_to_all | solution.py:77
  262.5 123.6 %all-reduce.3.cloned.1.call-done = bf16[512,8192]{1,0:T(8,128)(2,1)} async-done(((bf16[512,8192]{1,0:T(8,128)(2,1)}), bf16[512,8192]{1,0:T(8,128)(2,1)}) %all-reduce.3.cloned.1.call-update) | async-done | bytes 8388624 | tf_op jit(solution)/shard_map/psum | solution.py:66
  386.0 1.0 convert_convert_fusion
  387.0 0.9 reshape.75
  387.9 0.0 all-to-all-done.2
  387.9 7.0 %all-to-all-start.4 = ((bf16[8,2,8192]{2,1,0:T(2,128)(2,1)}), bf16[8,2,8192]{2,1,0:T(2,128)(2,1)S(1)}, u32[]{:S(2)}, u32[]{:S(2)}) async-start(bf16[8,2,8192]{2,1,0:T(2,128)(2,1)} %reshape.75), calls=%async_computation.4 | async-start | bytes 524288 | tf_op jit(solution)/shard_map/all_to_all | solution.py:70
  394.9 0.1 reshape.77
  395.0 0.7 select_reduce_fusion.1
  395.7 11.0 %all-to-all-done.4 = bf16[8,2,8192]{2,1,0:T(2,128)(2,1)S(1)} async-done(((bf16[8,2,8192]{2,1,0:T(2,128)(2,1)}), bf16[8,2,8192]{2,1,0:T(2,128)(2,1)S(1)}, u32[]{:S(2)}, u32[]{:S(2)}) %all-to-all-start.4) | async-done | bytes 262176 | tf_op jit(solution)/shard_map/all_to_all | solution.py:70
  406.7 0.1 reshape.76
  406.8 0.9 convolution_convert_fusion.2
  (3 shorter events, 0.0 us)
Async XLA Ops:
  7.2 1.6 copy-start
  7.2 88.0 %all-gather.4.cloned.1.call-start = ((), (), s32[]{:S(2)}) async-start(), calls=%async_computation.5 | async-start | bytes 8650752 | tf_op jit(solution)/shard_map/all_gather | solution.py:44
  31.0 10.9 %all-to-all-start.3 = ((bf16[8,1,2]{2,1,0:T(2,128)(2,1)}), bf16[8,1,2]{2,1,0:T(2,128)(2,1)S(1)}, u32[]{:S(2)}, u32[]{:S(2)}) async-start(bf16[8,1,2]{2,1,0:T(2,128)(2,1)} %convert_element_type.91), calls=%async_computation.3 | async-start | bytes 8192 | tf_op jit(solution)/shard_map/all_to_all | solution.py:41
  41.9 28.9 %all-to-all-start.1 = ((s32[8,1,2]{2,1,0:T(1,128)}), s32[8,1,2]{2,1,0:T(1,128)S(1)}, u32[]{:S(2)}, u32[]{:S(2)}) async-start(s32[8,1,2]{2,1,0:T(1,128)} %bitcast.2), calls=%async_computation.1 | async-start | bytes 8192 | tf_op jit(solution)/shard_map/all_to_all | solution.py:40
  45.3 340.8 %all-reduce.3.cloned.1.call-start = ((), (), s32[]{:S(2)}) async-start(), calls=%async_computation.6 | async-start | bytes 16777216 | tf_op jit(solution)/shard_map/psum | solution.py:66
  255.4 132.5 %all-to-all-start.2 = ((bf16[8,1,2]{2,1,0:T(2,128)(2,1)}), bf16[8,1,2]{2,1,0:T(2,128)(2,1)S(1)}, u32[]{:S(2)}, u32[]{:S(2)}) async-start(bf16[8,1,2]{2,1,0:T(2,128)(2,1)} %all_to_all.35), calls=%async_computation.2 | async-start | bytes 8192 | tf_op jit(solution)/shard_map/all_to_all | solution.py:77
  387.9 18.8 %all-to-all-start.4 = ((bf16[8,2,8192]{2,1,0:T(2,128)(2,1)}), bf16[8,2,8192]{2,1,0:T(2,128)(2,1)S(1)}, u32[]{:S(2)}, u32[]{:S(2)}) async-start(bf16[8,2,8192]{2,1,0:T(2,128)(2,1)} %reshape.75), calls=%async_computation.4 | async-start | bytes 524288 | tf_op jit(solution)/shard_map/all_to_all | solution.py:70
Sparse Core Ops, SparseCore 0:
  29.7 54.2 all-gather.3
  254.8 131.2 all-reduce.2
where the time goes:
time: 416 us; the launch traced here: 415 us
  blocking collectives  193 us (46%)
  waiting for transfers between devices  141 us (34%)
  matrix products  22.7 us (5%)
  starting transfers between devices  20.7 us (5%)
  local copies, waits for them, and re-layouts  17.3 us (4%)
  between operations  14.1 us (3%)
  other arithmetic  6.38 us (2%)
    psum x1, waiting for transfers between devices, per_device(): lax.psum(partial_value.astype(jnp.bfloat16), 'vocab').astype(jnp.float32)  124 us
    psum x1, blocking collectives, per_device(): row_total, target_logit = lax.psum((local_total, own_target), 'vocab')  62.7 us
    pmax x1, blocking collectives, per_device(): row_top = lax.pmax(jnp.max(logits, axis=1), 'vocab')  62 us
    all_gather x1, blocking collectives, per_device(): lax.all_gather(arrived[2], 'vocab', axis=0, tiled=True)  25 us
    all_gather x1, blocking collectives, per_device(): lax.all_gather(arrived[1], 'vocab', axis=0, tiled=True)  22.7 us
    all_to_all x1, blocking collectives, per_device(): lax.all_to_all(send_rows, 'head', split_axis=0, concat_axis=0, tiled=True)  20.2 us
    reshape x1, local copies, waits for them, and re-layouts, per_device(): gathered = grouped[0].reshape(-1, hidden_states.shape[1])  13.1 us
    dot_general x1, matrix products, per_device(): logits = jnp.dot(gathered, weight, preferred_element_type=jnp.float32)  11 us
  transfers between devices with their start and end apart: 6, of which 3 were waited for; matrix products, arithmetic and copies ran while one was open for 2% of the time, Pallas kernels for 0%

commit v1 on v0

v1 whole, which is shorter than its diff:
```python
import jax
import jax.numpy as jnp
from jax import lax
from jax.sharding import PartitionSpec as P

CAP = 2
META = 128


def per_device(hidden_states, head_weight, tags, targets, row_grad):
    head_count = lax.axis_size("head")
    own_rows = head_count * CAP
    width = hidden_states.shape[1]
    row_tag = tags[:, 0]
    local_rows = row_tag.shape[0]
    row_iota = lax.broadcasted_iota(jnp.int32, (local_rows, local_rows), 0)
    col_iota = lax.broadcasted_iota(jnp.int32, (local_rows, local_rows), 1)
    earlier = (row_tag[None, :] == row_tag[:, None]) & (col_iota < row_iota)
    slot_rank = jnp.sum(earlier.astype(jnp.int32), axis=1)
    slot_index = row_tag * CAP + slot_rank
    selector = jnp.arange(own_rows, dtype=jnp.int32)[:, None] == slot_index[None, :]

    meta_col = lax.broadcasted_iota(jnp.int32, (local_rows, META), 1)
    t = targets[:, None]
    meta = jnp.where(
        meta_col == 0,
        (t >> 7).astype(jnp.float32),
        jnp.where(
            meta_col == 1,
            (t & 127).astype(jnp.float32),
            jnp.where(meta_col == 2, row_grad[:, None].astype(jnp.float32), 0.0),
        ),
    ).astype(jnp.bfloat16)
    payload = jnp.concatenate([hidden_states, meta], axis=1)
    send = jnp.dot(
        selector.astype(jnp.bfloat16), payload, preferred_element_type=jnp.float32
    ).astype(jnp.bfloat16)

    arrived = lax.all_to_all(send, "head", split_axis=0, concat_axis=0, tiled=True)
    gathered = lax.all_gather(arrived, "vocab", axis=0, tiled=True)
    group_targets = (
        gathered[:, width].astype(jnp.int32) * 128 + gathered[:, width + 1].astype(jnp.int32)
    )
    group_scale = gathered[:, width + 2].astype(jnp.float32)

    weight = head_weight[0]
    vocab_width = weight.shape[1]
    logits = jnp.dot(gathered[:, :width], weight, preferred_element_type=jnp.float32)
    offset = lax.axis_index("vocab") * vocab_width
    target_hit = lax.broadcasted_iota(jnp.int32, logits.shape, 1) + offset == group_targets[:, None]
    own_target = jnp.sum(jnp.where(target_hit, logits, 0.0), axis=1)
    local_top = jnp.max(logits, axis=1)
    local_total = jnp.sum(jnp.exp(logits - local_top[:, None]), axis=1)
    stats = jnp.stack([local_top, local_total, own_target], axis=0)
    all_stats = lax.all_gather(stats, "vocab", axis=0, tiled=False)
    row_top = jnp.max(all_stats[:, 0, :], axis=0)
    row_total = jnp.sum(all_stats[:, 1, :] * jnp.exp(all_stats[:, 0, :] - row_top[None, :]), axis=0)
    target_logit = jnp.sum(all_stats[:, 2, :], axis=0)
    group_loss = jnp.log(row_total) + row_top - target_logit
    probabilities = jnp.exp(logits - row_top[:, None]) / row_total[:, None]
    dlogits = (group_scale[:, None] * (probabilities - target_hit.astype(jnp.float32))).astype(
        jnp.bfloat16
    )
    partial_value = lax.dot_general(
        dlogits, weight, (((1,), (1,)), ((), ())), preferred_element_type=jnp.float32
    ).astype(jnp.bfloat16)
    own_grad = lax.psum_scatter(partial_value, "vocab", scatter_dimension=0, tiled=True)
    own_loss = lax.dynamic_slice_in_dim(group_loss, lax.axis_index("vocab") * own_rows, own_rows, 0)
    back_meta = jnp.where(
        lax.broadcasted_iota(jnp.int32, (own_rows, META), 1) == 0, own_loss[:, None], 0.0
    ).astype(jnp.bfloat16)
    back = jnp.concatenate([own_grad, back_meta], axis=1)
    returned = lax.all_to_all(back, "head", split_axis=0, concat_axis=0, tiled=True)
    restored = jnp.dot(
        selector.T.astype(jnp.bfloat16), returned, preferred_element_type=jnp.float32
    ).astype(jnp.bfloat16)
    hidden_grad = restored[:, :width]
    row_loss = restored[:, width]
    return (row_loss, hidden_grad)


def solution(mesh):
    placed = (
        P(("head", "vocab"), None),
        P("head", None, "vocab"),
        P(("head", "vocab"), None),
        P(("head", "vocab")),
        P(("head", "vocab")),
    )
    return jax.shard_map(
        per_device,
        mesh=mesh,
        in_specs=placed,
        out_specs=(P(("head", "vocab")), P(("head", "vocab"), None)),
        check_vma=False,
    )
```

time: 416 us -> 262 us (0.63)
  blocking collectives: 193 us -> 61 us
  starting transfers between devices: 20.7 us -> 0.08 us
  local copies, waits for them, and re-layouts: 17.3 us -> 2.51 us
  waiting for transfers between devices: 141 us -> 155 us
    psum x1 -> x0, waiting for transfers between devices: 124 us -> none  [per_device(): lax.psum(partial_value.astype(jnp.bfloat16), 'vocab').astype(jnp.float32)]
    reduce_scatter x0 -> x1, waiting for transfers between devices: none -> 100 us  [per_device(): lax.psum_scatter(partial_value, 'vocab', scatter_dimension=0, tiled=True)]
    psum x1 -> x0, blocking collectives: 62.7 us -> none  [per_device(): row_total, target_logit = lax.psum((local_total, own_target), 'vocab')]
    pmax x1 -> x0, blocking collectives: 62 us -> none  [per_device(): row_top = lax.pmax(jnp.max(logits, axis=1), 'vocab')]
    all_gather x1, waiting for transfers between devices: 0.02 us -> 54.5 us  [per_device(): gathered = lax.all_gather(arrived, 'vocab', axis=0, tiled=True)]
    all_gather x2 -> x1, blocking collectives: 47.6 us -> 23.3 us  [per_device(): all_stats = lax.all_gather(stats, 'vocab', axis=0, tiled=False)]
    all_to_all x4 -> x0, starting transfers between devices: 20.6 us -> none  [the longest x1 7.05 us: per_device(): lax.all_to_all(own_loss.reshape(head_count, CAP), 'head', split_axis=0, c...]
    all_to_all x1 -> x2, blocking collectives: 20.2 us -> 37.7 us  [the longest x1 20.3 us: per_device(): lax.all_to_all(send, 'head', split_axis=0, concat_axis=0, tiled=True)]
  transfers between devices with their start and end apart: 6 -> 2, of which waited for: 3 -> 2; matrix products, arithmetic and copies ran while one was open for 2% -> 0% of each run, Pallas kernels for 0% -> 0%
where the time goes in v1:
time: 262 us
  waiting for transfers between devices  155 us (59%)
  blocking collectives  61 us (23%)
  matrix products  22.8 us (9%)
  between operations  14.1 us (5%)
  other arithmetic  6.83 us (3%)
    reduce_scatter x1, waiting for transfers between devices, per_device(): lax.psum_scatter(partial_value, 'vocab', scatter_dimension=0, tiled=True)  100 us
    all_gather x1, waiting for transfers between devices, per_device(): gathered = lax.all_gather(arrived, 'vocab', axis=0, tiled=True)  54.5 us
    all_gather x1, blocking collectives, per_device(): all_stats = lax.all_gather(stats, 'vocab', axis=0, tiled=False)  23.3 us
    all_to_all x1, blocking collectives, per_device(): lax.all_to_all(send, 'head', split_axis=0, concat_axis=0, tiled=True)  20.3 us
    all_to_all x1, blocking collectives, per_device(): lax.all_to_all(back, 'head', split_axis=0, concat_axis=0, tiled=True)  17.4 us
    dot_general x1, matrix products, per_device(): jnp.dot(gathered[:, :width], weight, preferred_element_type=jnp.float32)  11 us
    dot_general x1, matrix products, per_device(): lax.dot_general(dlogits, weight, (((1,), (1,)), ((), ())), preferred_elem...  10.5 us
  transfers between devices with their start and end apart: 2, of which 2 were waited for; matrix products, arithmetic and copies ran while one was open for 0% of the time, Pallas kernels for 0%

profile of v1, /device:TPU:2, one launch (start us, length us, event | category | flops | bytes accessed | tf_op | source)
XLA Modules:
  0.0 261.9 jit_solution(17612904875394351494)
XLA Ops:
  7.2 0.0 all-gather.4.cloned.1.call-start
  7.2 0.9 convert_reduce_fusion.1
  8.1 0.7 multiply_add_fusion
  8.8 0.7 shift-right-arithmetic_convert_fusion
  9.5 0.7 select_convert_fusion.1
  10.2 1.1 convolution_convert_fusion.1
  11.3 0.1 all_to_all.16
  11.4 20.3 %all_to_all.24 = bf16[8,2,8320]{2,1,0:T(2,128)(2,1)S(1)} all-to-all(bf16[8,2,8320]{2,1,0:T(2,128)(2,1)S(1)} %all_to_all.16), channel_id=1, replica_groups=mesh['head'=8,'vocab'=32] {'head'}, dimensions={0} | all-to-all | bytes 532480 | tf_op jit(solution)/shard_map/all_to_all | solution.py:39
  31.7 0.8 all_to_all.18
  32.6 0.0 all-gather.4.cloned.1.call-update
  32.6 0.0 reduce-scatter.2.cloned.1.call-start
  32.7 54.5 %all-gather.4.cloned.1.call-done = bf16[512,8320]{1,0:T(8,128)(2,1)} async-done(((bf16[16,8320]{1,0:T(8,128)(2,1)}), bf16[512,8320]{1,0:T(8,128)(2,1)}) %all-gather.4.cloned.1.call-update) | async-done | bytes 8519696 | tf_op jit(solution)/shard_map/all_gather | solution.py:40
  87.1 1.2 add_reduce_fusion
  88.4 11.0 %fusion.26 = (f32[512]{0:T(512)S(1)}, f32[512,512]{0,1:T(8,128)S(1)}) fusion(bf16[1,8192,512]{2,1,0:T(8,128)(2,1)} %param.6, bf16[512,8320]{1,0:T(8,128)(2,1)} %all-gather.4.cloned.1.call-done), kind=kOutput, calls=%fused_computation.52 | convolution fusion | flops 4295228928 | bytes 17827840 | tf_op jit(solution)/shard_map/dot_general | solution.py:48
  99.4 0.3 exponential_reduce_fusion
  99.6 23.3 %all-gather.1 = f32[32,3,512]{2,1,0:T(4,128)S(1)} all-gather(f32[1,3,512]{2,1,0:T(4,128)S(1)} %maximum_bitcast_fusion), channel_id=2, replica_groups=mesh['head'=8,'vocab'=32] {'vocab'}, dimensions={0}, use_global_device_ids=true | all-gather | bytes 202752 | tf_op jit(solution)/shard_map/all_gather | solution.py:55
  122.9 0.2 fusion.25
  123.1 1.1 convert_reduce_fusion
  124.2 10.5 %convolution_convert_fusion = bf16[512,8192]{1,0:T(8,128)(2,1)} fusion(bf16[1,8192,512]{2,1,0:T(8,128)(2,1)} %param.6, f32[512,512]{0,1:T(8,128)S(1)} %get-tuple-element.13, f32[512]{0:T(512)S(1)} %fusion.20, f32[512]{0:T(512)S(1)} %get-tuple-element.9, s32[512]{0:T(512)S(1)} %add_reduce_fusion, f32[512]{0:T(512)S(1)} %convert_reduce_fusion, ...), kind=kOutput, calls=%fused_computation | convolution fusion | flops 4300996608 | bytes 17836032 | tf_op jit(solution)/shard_map/dot_general | solution.py:64
  134.7 0.0 reduce-scatter.2.cloned.1.call-update
  134.7 0.1 dynamic_slice.3
  134.8 0.1 select_convert_fusion
  134.9 100.1 %reduce-scatter.2.cloned.1.call-done = bf16[16,8192]{1,0:T(8,128)(2,1)} async-done(((bf16[512,8192]{1,0:T(8,128)(2,1)}), bf16[16,8192]{1,0:T(8,128)(2,1)}) %reduce-scatter.2.cloned.1.call-update) | async-done | bytes 262160 | tf_op jit(solution)/shard_map/reduce_scatter | solution.py:67
  235.0 1.0 pad_maximum_fusion
  235.9 0.1 all_to_all.19
  236.0 17.4 %all_to_all.25 = bf16[8,2,8320]{2,1,0:T(2,128)(2,1)S(1)} all-to-all(bf16[8,2,8320]{2,1,0:T(2,128)(2,1)S(1)} %all_to_all.19), channel_id=1, replica_groups=mesh['head'=8,'vocab'=32] {'head'}, dimensions={0} | all-to-all | bytes 532480 | tf_op jit(solution)/shard_map/all_to_all | solution.py:73
  253.5 0.1 all_to_all.21
  253.6 0.2 convolution_convert_fusion.2
  253.8 0.6 slice_reduce_fusion.1
  254.4 0.7 slice.45
  (6 shorter events, 0.1 us)
Async XLA Ops:
  7.2 80.0 %all-gather.4.cloned.1.call-start = ((), (), s32[]{:S(2)}) async-start(), calls=%async_computation.3 | async-start | bytes 8785920 | tf_op jit(solution)/shard_map/all_gather | solution.py:40
  32.6 202.4 %reduce-scatter.2.cloned.1.call-start = ((), (), s32[]{:S(2)}) async-start(), calls=%async_computation.4 | async-start | bytes 8650752 | tf_op jit(solution)/shard_map/reduce_scatter | solution.py:67
Sparse Core Ops, SparseCore 0:
  32.7 54.3 all-gather.3
  134.8 100.0 reduce-scatter.1

commit v2 on v1

--- a/solution.py
+++ b/solution.py
@@ -37,7 +37,8 @@
     ).astype(jnp.bfloat16)
 
     arrived = lax.all_to_all(send, "head", split_axis=0, concat_axis=0, tiled=True)
-    gathered = lax.all_gather(arrived, "vocab", axis=0, tiled=True)
+    gathered = lax.all_gather(arrived, "chip", axis=0, tiled=True)
+    gathered = lax.all_gather(gathered, "core", axis=0, tiled=True)
     group_targets = (
         gathered[:, width].astype(jnp.int32) * 128 + gathered[:, width + 1].astype(jnp.int32)
     )
@@ -46,13 +47,14 @@
     weight = head_weight[0]
     vocab_width = weight.shape[1]
     logits = jnp.dot(gathered[:, :width], weight, preferred_element_type=jnp.float32)
-    offset = lax.axis_index("vocab") * vocab_width
+    vocab_index = lax.axis_index("chip") * lax.axis_size("core") + lax.axis_index("core")
+    offset = vocab_index * vocab_width
     target_hit = lax.broadcasted_iota(jnp.int32, logits.shape, 1) + offset == group_targets[:, None]
     own_target = jnp.sum(jnp.where(target_hit, logits, 0.0), axis=1)
     local_top = jnp.max(logits, axis=1)
     local_total = jnp.sum(jnp.exp(logits - local_top[:, None]), axis=1)
     stats = jnp.stack([local_top, local_total, own_target], axis=0)
-    all_stats = lax.all_gather(stats, "vocab", axis=0, tiled=False)
+    all_stats = lax.all_gather(stats, ("chip", "core"), axis=0, tiled=False)
     row_top = jnp.max(all_stats[:, 0, :], axis=0)
     row_total = jnp.sum(all_stats[:, 1, :] * jnp.exp(all_stats[:, 0, :] - row_top[None, :]), axis=0)
     target_logit = jnp.sum(all_stats[:, 2, :], axis=0)
@@ -64,8 +66,10 @@
     partial_value = lax.dot_general(
         dlogits, weight, (((1,), (1,)), ((), ())), preferred_element_type=jnp.float32
     ).astype(jnp.bfloat16)
-    own_grad = lax.psum_scatter(partial_value, "vocab", scatter_dimension=0, tiled=True)
-    own_loss = lax.dynamic_slice_in_dim(group_loss, lax.axis_index("vocab") * own_rows, own_rows, 0)
+    half = lax.psum_scatter(partial_value, "core", scatter_dimension=0, tiled=True)
+    own_grad = lax.psum_scatter(half, "chip", scatter_dimension=0, tiled=True)
+    own_start = (lax.axis_index("core") * lax.axis_size("chip") + lax.axis_index("chip")) * own_rows
+    own_loss = lax.dynamic_slice_in_dim(group_loss, own_start, own_rows, 0)
     back_meta = jnp.where(
         lax.broadcasted_iota(jnp.int32, (own_rows, META), 1) == 0, own_loss[:, None], 0.0
     ).astype(jnp.bfloat16)
@@ -80,17 +84,20 @@
 
 
 def solution(mesh):
+    heads, vocab = mesh.devices.shape
+    split = jax.sharding.Mesh(mesh.devices.reshape(heads, vocab // 2, 2), ("head", "chip", "core"))
+    rows = ("head", "chip", "core")
     placed = (
-        P(("head", "vocab"), None),
-        P("head", None, "vocab"),
-        P(("head", "vocab"), None),
-        P(("head", "vocab")),
-        P(("head", "vocab")),
+        P(rows, None),
+        P("head", None, ("chip", "core")),
+        P(rows, None),
+        P(rows),
+        P(rows),
     )
     return jax.shard_map(
         per_device,
-        mesh=mesh,
+        mesh=split,
         in_specs=placed,
-        out_specs=(P(("head", "vocab")), P(("head", "vocab"), None)),
+        out_specs=(P(rows), P(rows, None)),
         check_vma=False,
     )

time: 262 us -> 299 us (1.14)
  waiting for transfers between devices: 155 us -> 190 us
    all_gather x1 -> x2, waiting for transfers between devices: 54.5 us -> 80.7 us  [the longest x1 53.2 us: per_device(): gathered = lax.all_gather(arrived, 'chip', axis=0, tiled=True)]
    reduce_scatter x1 -> x2, waiting for transfers between devices: 100 us -> 109 us  [the longest x1 87.9 us: per_device(): own_grad = lax.psum_scatter(half, 'chip', scatter_dimension=0, tiled=True)]
  transfers between devices with their start and end apart: 2 -> 4, of which waited for: 2 -> 4; matrix products, arithmetic and copies ran while one was open for 0% -> 0% of each run, Pallas kernels for 0% -> 0%
where the time goes in v2:
time: 299 us
  waiting for transfers between devices  190 us (64%)
  blocking collectives  62.3 us (21%)
  matrix products  22.8 us (8%)
  between operations  13.9 us (5%)
  other arithmetic  6.83 us (2%)
    reduce_scatter x1, waiting for transfers between devices, per_device(): own_grad = lax.psum_scatter(half, 'chip', scatter_dimension=0, tiled=True)  87.9 us
    all_gather x1, waiting for transfers between devices, per_device(): gathered = lax.all_gather(arrived, 'chip', axis=0, tiled=True)  53.2 us
    all_gather x1, waiting for transfers between devices, per_device(): gathered = lax.all_gather(gathered, 'core', axis=0, tiled=True)  27.6 us
    all_gather x1, blocking collectives, per_device(): all_stats = lax.all_gather(stats, ('chip', 'core'), axis=0, tiled=False)  24.6 us
    reduce_scatter x1, waiting for transfers between devices, per_device(): lax.psum_scatter(partial_value, 'core', scatter_dimension=0, tiled=True)  21.6 us
    all_to_all x1, blocking collectives, per_device(): lax.all_to_all(send, 'head', split_axis=0, concat_axis=0, tiled=True)  20.3 us
    all_to_all x1, blocking collectives, per_device(): lax.all_to_all(back, 'head', split_axis=0, concat_axis=0, tiled=True)  17.4 us
    dot_general x1, matrix products, per_device(): jnp.dot(gathered[:, :width], weight, preferred_element_type=jnp.float32)  11 us
  transfers between devices with their start and end apart: 4, of which 4 were waited for; matrix products, arithmetic and copies ran while one was open for 0% of the time, Pallas kernels for 0%

profile of v2, /device:TPU:2, one launch (start us, length us, event | category | flops | bytes accessed | tf_op | source)
XLA Modules:
  0.0 298.7 jit_solution(13257573625504628582)
XLA Ops:
  7.2 0.0 all-gather.5.cloned.1.call-start
  7.2 0.7 shift-right-arithmetic_convert_fusion
  7.9 0.9 convert_reduce_fusion.1
  8.8 0.7 multiply_add_fusion
  9.5 0.7 select_convert_fusion.1
  10.2 1.1 convolution_convert_fusion.1
  11.3 0.1 all_to_all.16
  11.4 20.3 %all_to_all.24 = bf16[8,2,8320]{2,1,0:T(2,128)(2,1)S(1)} all-to-all(bf16[8,2,8320]{2,1,0:T(2,128)(2,1)S(1)} %all_to_all.16), channel_id=1, replica_groups=mesh['head'=8,'chip'=16,'core'=2] {'head'}, dimensions={0} | all-to-all | bytes 532480 | tf_op jit(solution)/shard_map/all_to_all | solution.py:39
  31.7 0.8 all_to_all.18
  32.5 0.0 all-gather.5.cloned.1.call-update
  32.6 0.0 all-gather.7.cloned.1.call-start
  32.6 53.2 %all-gather.5.cloned.1.call-done = bf16[256,8320]{1,0:T(8,128)(2,1)} async-done(((bf16[16,8320]{1,0:T(8,128)(2,1)}), bf16[256,8320]{1,0:T(8,128)(2,1)}) %all-gather.5.cloned.1.call-update) | async-done | bytes 4259856 | tf_op jit(solution)/shard_map/all_gather | solution.py:40
  85.8 0.0 all-gather.7.cloned.1.call-update
  85.8 0.0 reduce-scatter.3.cloned.1.call-start
  85.9 27.6 %all-gather.7.cloned.1.call-done = bf16[512,8320]{1,0:T(8,128)(2,1)} async-done(((bf16[256,8320]{1,0:T(8,128)(2,1)}), bf16[512,8320]{1,0:T(8,128)(2,1)}) %all-gather.7.cloned.1.call-update) | async-done | bytes 8519696 | tf_op jit(solution)/shard_map/all_gather | solution.py:41
  113.4 1.2 add_reduce_fusion
  114.6 11.0 %fusion.26 = (f32[512]{0:T(512)S(1)}, f32[512,512]{0,1:T(8,128)S(1)}) fusion(bf16[1,8192,512]{2,1,0:T(8,128)(2,1)} %param.6, bf16[512,8320]{1,0:T(8,128)(2,1)} %all-gather.7.cloned.1.call-done), kind=kOutput, calls=%fused_computation.52 | convolution fusion | flops 4295228928 | bytes 17827840 | tf_op jit(solution)/shard_map/dot_general | solution.py:49
  125.7 0.3 exponential_reduce_fusion
  125.9 24.6 %all-gather.1 = f32[32,3,512]{2,1,0:T(4,128)S(1)} all-gather(f32[1,3,512]{2,1,0:T(4,128)S(1)} %maximum_bitcast_fusion), channel_id=2, replica_groups=mesh['head'=8,'chip'=16,'core'=2] {'chip','core'}, dimensions={0}, use_global_device_ids=true | all-gather | bytes 202752 | tf_op jit(solution)/shard_map/all_gather | solution.py:57
  150.5 0.2 fusion.25
  150.7 1.1 convert_reduce_fusion
  151.8 10.5 %convolution_convert_fusion = bf16[512,8192]{1,0:T(8,128)(2,1)} fusion(bf16[1,8192,512]{2,1,0:T(8,128)(2,1)} %param.6, f32[512,512]{0,1:T(8,128)S(1)} %get-tuple-element.13, f32[512]{0:T(512)S(1)} %fusion.20, f32[512]{0:T(512)S(1)} %get-tuple-element.9, s32[512]{0:T(512)S(1)} %add_reduce_fusion, f32[512]{0:T(512)S(1)} %convert_reduce_fusion, ...), kind=kOutput, calls=%fused_computation | convolution fusion | flops 4300996608 | bytes 17836032 | tf_op jit(solution)/shard_map/dot_general | solution.py:66
  162.3 0.0 reduce-scatter.3.cloned.1.call-update
  162.3 0.0 reduce-scatter.5.cloned.1.call-start
  162.3 21.6 %reduce-scatter.3.cloned.1.call-done = bf16[256,8192]{1,0:T(8,128)(2,1)} async-done(((bf16[512,8192]{1,0:T(8,128)(2,1)}), bf16[256,8192]{1,0:T(8,128)(2,1)}) %reduce-scatter.3.cloned.1.call-update) | async-done | bytes 4194320 | tf_op jit(solution)/shard_map/reduce_scatter | solution.py:69
  183.9 0.0 reduce-scatter.5.cloned.1.call-update
  184.0 0.1 dynamic_slice.3
  184.1 0.1 select_convert_fusion
  184.2 87.9 %reduce-scatter.5.cloned.1.call-done = bf16[16,8192]{1,0:T(8,128)(2,1)} async-done(((bf16[256,8192]{1,0:T(8,128)(2,1)}), bf16[16,8192]{1,0:T(8,128)(2,1)}) %reduce-scatter.5.cloned.1.call-update) | async-done | bytes 262160 | tf_op jit(solution)/shard_map/reduce_scatter | solution.py:70
  272.0 1.0 pad_maximum_fusion
  273.0 0.1 all_to_all.19
  273.1 17.4 %all_to_all.25 = bf16[8,2,8320]{2,1,0:T(2,128)(2,1)S(1)} all-to-all(bf16[8,2,8320]{2,1,0:T(2,128)(2,1)S(1)} %all_to_all.19), channel_id=1, replica_groups=mesh['head'=8,'chip'=16,'core'=2] {'head'}, dimensions={0} | all-to-all | bytes 532480 | tf_op jit(solution)/shard_map/all_to_all | solution.py:77
  290.5 0.1 all_to_all.21
  290.6 0.2 convolution_convert_fusion.2
  290.9 0.7 slice.45
  291.5 0.6 slice_reduce_fusion.1
  (6 shorter events, 0.1 us)
Async XLA Ops:
  7.2 78.6 %all-gather.5.cloned.1.call-start = ((), (), s32[]{:S(2)}) async-start(), calls=%async_computation.4 | async-start | bytes 4526080 | tf_op jit(solution)/shard_map/all_gather | solution.py:40
  32.6 80.9 %all-gather.7.cloned.1.call-start = ((), (), s32[]{:S(2)}) async-start(), calls=%async_computation.5 | async-start | bytes 12779520 | tf_op jit(solution)/shard_map/all_gather | solution.py:41
  85.8 98.1 %reduce-scatter.3.cloned.1.call-start = ((), (), s32[]{:S(2)}) async-start(), calls=%async_computation.6 | async-start | bytes 12582912 | tf_op jit(solution)/shard_map/reduce_scatter | solution.py:69
  162.3 109.7 %reduce-scatter.5.cloned.1.call-start = ((), (), s32[]{:S(2)}) async-start(), calls=%async_computation.7 | async-start | bytes 4456448 | tf_op jit(solution)/shard_map/reduce_scatter | solution.py:70
Sparse Core Ops, SparseCore 0:
  32.7 53.0 all-gather.4
  87.6 25.8 all-gather.6
  162.4 21.4 reduce-scatter.2
  187.4 84.5 reduce-scatter.4

commit v3 on v1

--- a/solution.py
+++ b/solution.py
@@ -52,7 +52,8 @@
     local_top = jnp.max(logits, axis=1)
     local_total = jnp.sum(jnp.exp(logits - local_top[:, None]), axis=1)
     stats = jnp.stack([local_top, local_total, own_target], axis=0)
-    all_stats = lax.all_gather(stats, "vocab", axis=0, tiled=False)
+    copies = jnp.broadcast_to(stats[None], (lax.axis_size("vocab"),) + stats.shape)
+    all_stats = lax.all_to_all(copies, "vocab", split_axis=0, concat_axis=0, tiled=True)
     row_top = jnp.max(all_stats[:, 0, :], axis=0)
     row_total = jnp.sum(all_stats[:, 1, :] * jnp.exp(all_stats[:, 0, :] - row_top[None, :]), axis=0)
     target_logit = jnp.sum(all_stats[:, 2, :], axis=0)

time: 262 us -> 251 us (0.958)
  blocking collectives: 61 us -> 37.7 us
  starting transfers between devices: 0.08 us -> 5.86 us
  waiting for transfers between devices: 155 us -> 160 us
    all_gather x1 -> x0, blocking collectives: 23.3 us -> none  [per_device(): all_stats = lax.all_gather(stats, 'vocab', axis=0, tiled=False)]
    all_to_all x0 -> x1, waiting for transfers between devices: none -> 6.41 us  [per_device(): lax.all_to_all(copies, 'vocab', split_axis=0, concat_axis=0, tiled=True)]
    all_to_all x0 -> x1, starting transfers between devices: none -> 5.78 us  [per_device(): lax.all_to_all(copies, 'vocab', split_axis=0, concat_axis=0, tiled=True)]
  transfers between devices with their start and end apart: 2 -> 3, of which waited for: 2 -> 3; matrix products, arithmetic and copies ran while one was open for 0% -> 1% of each run, Pallas kernels for 0% -> 0%
where the time goes in v3:
time: 251 us
  waiting for transfers between devices  160 us (64%)
  blocking collectives  37.7 us (15%)
  matrix products  22.8 us (9%)
  between operations  14.1 us (6%)
  other arithmetic  6.83 us (3%)
  starting transfers between devices  5.86 us (2%)
  local copies, waits for them, and re-layouts  3.27 us (1%)
    reduce_scatter x1, waiting for transfers between devices, per_device(): lax.psum_scatter(partial_value, 'vocab', scatter_dimension=0, tiled=True)  99 us
    all_gather x1, waiting for transfers between devices, per_device(): gathered = lax.all_gather(arrived, 'vocab', axis=0, tiled=True)  54.5 us
    all_to_all x1, blocking collectives, per_device(): lax.all_to_all(send, 'head', split_axis=0, concat_axis=0, tiled=True)  20.3 us
    all_to_all x1, blocking collectives, per_device(): lax.all_to_all(back, 'head', split_axis=0, concat_axis=0, tiled=True)  17.4 us
    dot_general x1, matrix products, per_device(): jnp.dot(gathered[:, :width], weight, preferred_element_type=jnp.float32)  11 us
    dot_general x1, matrix products, per_device(): lax.dot_general(dlogits, weight, (((1,), (1,)), ((), ())), preferred_elem...  10.4 us
    all_to_all x1, waiting for transfers between devices, per_device(): lax.all_to_all(copies, 'vocab', split_axis=0, concat_axis=0, tiled=True)  6.41 us
    all_to_all x1, starting transfers between devices, per_device(): lax.all_to_all(copies, 'vocab', split_axis=0, concat_axis=0, tiled=True)  5.78 us
  transfers between devices with their start and end apart: 3, of which 3 were waited for; matrix products, arithmetic and copies ran while one was open for 1% of the time, Pallas kernels for 0%

profile of v3, /device:TPU:2, one launch (start us, length us, event | category | flops | bytes accessed | tf_op | source)
XLA Modules:
  0.0 250.6 jit_solution(10200066326224845656)
XLA Ops:
  7.2 0.0 all-gather.2.cloned.1.call-start
  7.2 0.9 convert_reduce_fusion.1
  8.1 0.7 multiply_add_fusion
  8.8 0.7 shift-right-arithmetic_convert_fusion
  9.5 0.7 select_convert_fusion.1
  10.2 1.1 convolution_convert_fusion.1
  11.3 0.1 all_to_all.19
  11.4 20.3 %all_to_all.29 = bf16[8,2,8320]{2,1,0:T(2,128)(2,1)S(1)} all-to-all(bf16[8,2,8320]{2,1,0:T(2,128)(2,1)S(1)} %all_to_all.19), channel_id=1, replica_groups=mesh['head'=8,'vocab'=32] {'head'}, dimensions={0} | all-to-all | bytes 532480 | tf_op jit(solution)/shard_map/all_to_all | solution.py:39
  31.7 0.8 all_to_all.21
  32.6 0.0 all-gather.2.cloned.1.call-update
  32.6 54.5 %all-gather.2.cloned.1.call-done = bf16[512,8320]{1,0:T(8,128)(2,1)} async-done(((bf16[16,8320]{1,0:T(8,128)(2,1)}), bf16[512,8320]{1,0:T(8,128)(2,1)}) %all-gather.2.cloned.1.call-update) | async-done | bytes 8519696 | tf_op jit(solution)/shard_map/all_gather | solution.py:40
  87.1 1.2 add_reduce_fusion
  88.4 11.0 %fusion.25 = (f32[512]{0:T(512)S(1)}, f32[512,512]{0,1:T(8,128)S(1)}) fusion(bf16[1,8192,512]{2,1,0:T(8,128)(2,1)} %param.6, bf16[512,8320]{1,0:T(8,128)(2,1)} %all-gather.2.cloned.1.call-done), kind=kOutput, calls=%fused_computation.51 | convolution fusion | flops 4295228928 | bytes 17827840 | tf_op jit(solution)/shard_map/dot_general | solution.py:48
  99.4 0.3 exponential_reduce_fusion
  99.7 0.8 broadcast_in_dim.63
  100.4 5.8 %all-to-all-start.1 = ((f32[32,3,512]{2,1,0:T(4,128)}), f32[32,3,512]{2,1,0:T(4,128)S(1)}, u32[]{:S(2)}, u32[]{:S(2)}) async-start(f32[32,3,512]{2,1,0:T(4,128)} %broadcast_in_dim.63), calls=%async_computation.1 | async-start | bytes 524288 | tf_op jit(solution)/shard_map/all_to_all | solution.py:56
  106.2 0.0 reduce-scatter.2.cloned.1.call-start
  106.2 1.1 convert_reduce_fusion
  107.4 6.4 %all-to-all-done.1 = f32[32,3,512]{2,1,0:T(4,128)S(1)} async-done(((f32[32,3,512]{2,1,0:T(4,128)}), f32[32,3,512]{2,1,0:T(4,128)S(1)}, u32[]{:S(2)}, u32[]{:S(2)}) %all-to-all-start.1) | async-done | bytes 196640 | tf_op jit(solution)/shard_map/all_to_all | solution.py:56
  113.8 0.2 slice_reduce_fusion.2
  114.0 10.4 %convolution_convert_fusion = bf16[512,8192]{1,0:T(8,128)(2,1)} fusion(bf16[1,8192,512]{2,1,0:T(8,128)(2,1)} %param.6, f32[512,512]{0,1:T(8,128)S(1)} %get-tuple-element.11, f32[512]{0:T(512)S(1)} %fusion.20, f32[512]{0:T(512)S(1)} %get-tuple-element.4, s32[512]{0:T(512)S(1)} %add_reduce_fusion, f32[512]{0:T(512)S(1)} %convert_reduce_fusion, ...), kind=kOutput, calls=%fused_computation | convolution fusion | flops 4300996608 | bytes 17836032 | tf_op jit(solution)/shard_map/dot_general | solution.py:65
  124.4 0.0 reduce-scatter.2.cloned.1.call-update
  124.5 0.1 dynamic_slice.3
  124.6 0.1 select_convert_fusion
  124.6 99.0 %reduce-scatter.2.cloned.1.call-done = bf16[16,8192]{1,0:T(8,128)(2,1)} async-done(((bf16[512,8192]{1,0:T(8,128)(2,1)}), bf16[16,8192]{1,0:T(8,128)(2,1)}) %reduce-scatter.2.cloned.1.call-update) | async-done | bytes 262160 | tf_op jit(solution)/shard_map/reduce_scatter | solution.py:68
  223.6 1.0 pad_maximum_fusion
  224.6 0.1 all_to_all.23
  224.7 17.4 %all_to_all.30 = bf16[8,2,8320]{2,1,0:T(2,128)(2,1)S(1)} all-to-all(bf16[8,2,8320]{2,1,0:T(2,128)(2,1)S(1)} %all_to_all.23), channel_id=1, replica_groups=mesh['head'=8,'vocab'=32] {'head'}, dimensions={0} | all-to-all | bytes 532480 | tf_op jit(solution)/shard_map/all_to_all | solution.py:74
  242.1 0.1 all_to_all.25
  242.2 0.2 convolution_convert_fusion.2
  242.5 0.6 slice_reduce_fusion.1
  243.1 0.7 slice.45
  (6 shorter events, 0.1 us)
Async XLA Ops:
  7.2 80.0 %all-gather.2.cloned.1.call-start = ((), (), s32[]{:S(2)}) async-start(), calls=%async_computation.4 | async-start | bytes 8785920 | tf_op jit(solution)/shard_map/all_gather | solution.py:40
  100.4 13.4 %all-to-all-start.1 = ((f32[32,3,512]{2,1,0:T(4,128)}), f32[32,3,512]{2,1,0:T(4,128)S(1)}, u32[]{:S(2)}, u32[]{:S(2)}) async-start(f32[32,3,512]{2,1,0:T(4,128)} %broadcast_in_dim.63), calls=%async_computation.1 | async-start | bytes 524288 | tf_op jit(solution)/shard_map/all_to_all | solution.py:56
  106.2 117.4 %reduce-scatter.2.cloned.1.call-start = ((), (), s32[]{:S(2)}) async-start(), calls=%async_computation.5 | async-start | bytes 8650752 | tf_op jit(solution)/shard_map/reduce_scatter | solution.py:68
Sparse Core Ops, SparseCore 0:
  32.7 54.3 all-gather.1
  124.6 98.9 reduce-scatter.1

commit v4 on v3

--- a/solution.py
+++ b/solution.py
@@ -70,13 +70,14 @@
     back_meta = jnp.where(
         lax.broadcasted_iota(jnp.int32, (own_rows, META), 1) == 0, own_loss[:, None], 0.0
     ).astype(jnp.bfloat16)
-    back = jnp.concatenate([own_grad, back_meta], axis=1)
-    returned = lax.all_to_all(back, "head", split_axis=0, concat_axis=0, tiled=True)
-    restored = jnp.dot(
+    returned_meta = lax.all_to_all(back_meta, "head", split_axis=0, concat_axis=0, tiled=True)
+    row_loss = jnp.dot(
+        selector.T.astype(jnp.bfloat16), returned_meta, preferred_element_type=jnp.float32
+    ).astype(jnp.bfloat16)[:, 0]
+    returned = lax.all_to_all(own_grad, "head", split_axis=0, concat_axis=0, tiled=True)
+    hidden_grad = jnp.dot(
         selector.T.astype(jnp.bfloat16), returned, preferred_element_type=jnp.float32
     ).astype(jnp.bfloat16)
-    hidden_grad = restored[:, :width]
-    row_loss = restored[:, width]
     return (row_loss, hidden_grad)
 
 

time: 251 us -> 251 us (level)
  blocking collectives: 37.7 us -> 20.3 us
  starting transfers between devices: 5.86 us -> 19.9 us
    all_to_all x1 -> x0, blocking collectives: 17.4 us -> none  [per_device(): lax.all_to_all(back, 'head', split_axis=0, concat_axis=0, tiled=True)]
    all_to_all x0 -> x2, starting transfers between devices: none -> 14 us  [the longest x1 7.01 us: per_device(): lax.all_to_all(own_grad, 'head', split_axis=0, concat_axis=0, tiled=True)]
    all_to_all x0 -> x2, waiting for transfers between devices: none -> 9.67 us  [the longest x1 9.67 us: per_device(): lax.all_to_all(own_grad, 'head', split_axis=0, concat_axis=0, tiled=True)]
    reduce_scatter x1, waiting for transfers between devices: 99 us -> 91.3 us  [per_device(): lax.psum_scatter(partial_value, 'vocab', scatter_dimension=0, tiled=True)]
  transfers between devices with their start and end apart: 3 -> 5, of which waited for: 3 -> 4; matrix products, arithmetic and copies ran while one was open for 1% -> 1% of each run, Pallas kernels for 0% -> 0%
where the time goes in v4:
time: 251 us
  waiting for transfers between devices  162 us (65%)
  matrix products  23.6 us (9%)
  blocking collectives  20.3 us (8%)
  starting transfers between devices  19.9 us (8%)
  between operations  14.1 us (6%)
  other arithmetic  6.47 us (3%)
  local copies, waits for them, and re-layouts  4.42 us (2%)
    reduce_scatter x1, waiting for transfers between devices, per_device(): lax.psum_scatter(partial_value, 'vocab', scatter_dimension=0, tiled=True)  91.3 us
    all_gather x1, waiting for transfers between devices, per_device(): gathered = lax.all_gather(arrived, 'vocab', axis=0, tiled=True)  54.5 us
    all_to_all x1, blocking collectives, per_device(): lax.all_to_all(send, 'head', split_axis=0, concat_axis=0, tiled=True)  20.3 us
    dot_general x1, matrix products, per_device(): jnp.dot(gathered[:, :width], weight, preferred_element_type=jnp.float32)  11 us
    dot_general x1, matrix products, per_device(): lax.dot_general(dlogits, weight, (((1,), (1,)), ((), ())), preferred_elem...  10.5 us
    all_to_all x1, waiting for transfers between devices, per_device(): lax.all_to_all(own_grad, 'head', split_axis=0, concat_axis=0, tiled=True)  9.67 us
    all_to_all x1, starting transfers between devices, per_device(): lax.all_to_all(own_grad, 'head', split_axis=0, concat_axis=0, tiled=True)  7.01 us
    all_to_all x1, starting transfers between devices, per_device(): lax.all_to_all(back_meta, 'head', split_axis=0, concat_axis=0, tiled=True)  7.01 us
  transfers between devices with their start and end apart: 5, of which 4 were waited for; matrix products, arithmetic and copies ran while one was open for 1% of the time, Pallas kernels for 0%

profile of v4, /device:TPU:2, one launch (start us, length us, event | category | flops | bytes accessed | tf_op | source)
XLA Modules:
  0.0 250.8 jit_solution(11103800240023107871)
XLA Ops:
  7.2 0.0 all-gather.2.cloned.1.call-start
  7.2 0.9 convert_reduce_fusion.1
  8.1 0.7 multiply_add_fusion
  8.8 0.7 shift-right-arithmetic_convert_fusion
  9.5 0.7 select_convert_fusion.1
  10.2 1.1 convolution_convert_fusion.1
  11.3 0.1 all_to_all.25
  11.4 20.3 %all_to_all.38 = bf16[8,2,8320]{2,1,0:T(2,128)(2,1)S(1)} all-to-all(bf16[8,2,8320]{2,1,0:T(2,128)(2,1)S(1)} %all_to_all.25), channel_id=1, replica_groups=mesh['head'=8,'vocab'=32] {'head'}, dimensions={0} | all-to-all | bytes 532480 | tf_op jit(solution)/shard_map/all_to_all | solution.py:39
  31.7 0.8 all_to_all.27
  32.6 0.0 all-gather.2.cloned.1.call-update
  32.6 54.5 %all-gather.2.cloned.1.call-done = bf16[512,8320]{1,0:T(8,128)(2,1)} async-done(((bf16[16,8320]{1,0:T(8,128)(2,1)}), bf16[512,8320]{1,0:T(8,128)(2,1)}) %all-gather.2.cloned.1.call-update) | async-done | bytes 8519696 | tf_op jit(solution)/shard_map/all_gather | solution.py:40
  87.1 1.2 add_reduce_fusion
  88.4 11.0 %fusion.25 = (f32[512]{0:T(512)S(1)}, f32[512,512]{0,1:T(8,128)S(1)}) fusion(bf16[1,8192,512]{2,1,0:T(8,128)(2,1)} %param.6, bf16[512,8320]{1,0:T(8,128)(2,1)} %all-gather.2.cloned.1.call-done), kind=kOutput, calls=%fused_computation.52 | convolution fusion | flops 4295228928 | bytes 17827840 | tf_op jit(solution)/shard_map/dot_general | solution.py:48
  99.4 0.3 exponential_reduce_fusion
  99.7 0.8 broadcast_in_dim.65
  100.4 5.8 %all-to-all-start.1 = ((f32[32,3,512]{2,1,0:T(4,128)}), f32[32,3,512]{2,1,0:T(4,128)S(1)}, u32[]{:S(2)}, u32[]{:S(2)}) async-start(f32[32,3,512]{2,1,0:T(4,128)} %broadcast_in_dim.65), calls=%async_computation.1 | async-start | bytes 524288 | tf_op jit(solution)/shard_map/all_to_all | solution.py:56
  106.2 0.0 reduce-scatter.2.cloned.1.call-start
  106.2 1.1 convert_reduce_fusion
  107.4 6.4 %all-to-all-done.1 = f32[32,3,512]{2,1,0:T(4,128)S(1)} async-done(((f32[32,3,512]{2,1,0:T(4,128)}), f32[32,3,512]{2,1,0:T(4,128)S(1)}, u32[]{:S(2)}, u32[]{:S(2)}) %all-to-all-start.1) | async-done | bytes 196640 | tf_op jit(solution)/shard_map/all_to_all | solution.py:56
  113.8 0.2 slice_reduce_fusion.2
  114.0 10.5 %convolution_convert_fusion = bf16[512,8192]{1,0:T(8,128)(2,1)} fusion(bf16[1,8192,512]{2,1,0:T(8,128)(2,1)} %param.6, f32[512,512]{0,1:T(8,128)S(1)} %get-tuple-element.11, f32[512]{0:T(512)S(1)} %fusion.18, f32[512]{0:T(512)S(1)} %get-tuple-element.4, f32[512]{0:T(512)S(1)} %convert_reduce_fusion, s32[512]{0:T(512)S(1)} %add_reduce_fusion, ...), kind=kOutput, calls=%fused_computation | convolution fusion | flops 4300996608 | bytes 17836032 | tf_op jit(solution)/shard_map/dot_general | solution.py:65
  124.4 0.0 reduce-scatter.2.cloned.1.call-update
  124.5 0.1 dynamic_slice.3
  124.6 0.1 broadcast_in_dim.66
  124.6 0.7 select_convert_fusion
  125.3 7.0 %all-to-all-start.2 = ((bf16[8,2,128]{2,1,0:T(2,128)(2,1)}), bf16[8,2,128]{2,1,0:T(2,128)(2,1)S(1)}, u32[]{:S(2)}, u32[]{:S(2)}) async-start(bf16[8,2,128]{2,1,0:T(2,128)(2,1)} %select_convert_fusion), calls=%async_computation.2 | async-start | bytes 8192 | tf_op jit(solution)/shard_map/all_to_all | solution.py:73
  132.3 91.3 %reduce-scatter.2.cloned.1.call-done = bf16[16,8192]{1,0:T(8,128)(2,1)} async-done(((bf16[512,8192]{1,0:T(8,128)(2,1)}), bf16[16,8192]{1,0:T(8,128)(2,1)}) %reduce-scatter.2.cloned.1.call-update) | async-done | bytes 262160 | tf_op jit(solution)/shard_map/reduce_scatter | solution.py:68
  223.6 1.8 all_to_all.31
  225.4 0.0 all-to-all-done.2
  225.4 7.0 %all-to-all-start.3 = ((bf16[8,2,8192]{2,1,0:T(2,128)(2,1)}), bf16[8,2,8192]{2,1,0:T(2,128)(2,1)S(1)}, u32[]{:S(2)}, u32[]{:S(2)}) async-start(bf16[8,2,8192]{2,1,0:T(2,128)(2,1)} %all_to_all.31), calls=%async_computation.4 | async-start | bytes 524288 | tf_op jit(solution)/shard_map/all_to_all | solution.py:77
  232.5 0.2 convolution_convert_fusion.3
  232.6 0.6 slice_reduce_fusion.1
  233.3 9.7 %all-to-all-done.3 = bf16[8,2,8192]{2,1,0:T(2,128)(2,1)S(1)} async-done(((bf16[8,2,8192]{2,1,0:T(2,128)(2,1)}), bf16[8,2,8192]{2,1,0:T(2,128)(2,1)S(1)}, u32[]{:S(2)}, u32[]{:S(2)}) %all-to-all-start.3) | async-done | bytes 262176 | tf_op jit(solution)/shard_map/all_to_all | solution.py:77
  242.9 0.1 all_to_all.33
  243.0 0.9 convolution_convert_fusion.2
  (6 shorter events, 0.1 us)
Async XLA Ops:
  7.2 80.0 %all-gather.2.cloned.1.call-start = ((), (), s32[]{:S(2)}) async-start(), calls=%async_computation.5 | async-start | bytes 8785920 | tf_op jit(solution)/shard_map/all_gather | solution.py:40
  100.4 13.4 %all-to-all-start.1 = ((f32[32,3,512]{2,1,0:T(4,128)}), f32[32,3,512]{2,1,0:T(4,128)S(1)}, u32[]{:S(2)}, u32[]{:S(2)}) async-start(f32[32,3,512]{2,1,0:T(4,128)} %broadcast_in_dim.65), calls=%async_computation.1 | async-start | bytes 524288 | tf_op jit(solution)/shard_map/all_to_all | solution.py:56
  106.2 117.4 %reduce-scatter.2.cloned.1.call-start = ((), (), s32[]{:S(2)}) async-start(), calls=%async_computation.6 | async-start | bytes 8650752 | tf_op jit(solution)/shard_map/reduce_scatter | solution.py:68
  125.3 100.1 %all-to-all-start.2 = ((bf16[8,2,128]{2,1,0:T(2,128)(2,1)}), bf16[8,2,128]{2,1,0:T(2,128)(2,1)S(1)}, u32[]{:S(2)}, u32[]{:S(2)}) async-start(bf16[8,2,128]{2,1,0:T(2,128)(2,1)} %select_convert_fusion), calls=%async_computation.2 | async-start | bytes 8192 | tf_op jit(solution)/shard_map/all_to_all | solution.py:73
  225.4 17.5 %all-to-all-start.3 = ((bf16[8,2,8192]{2,1,0:T(2,128)(2,1)}), bf16[8,2,8192]{2,1,0:T(2,128)(2,1)S(1)}, u32[]{:S(2)}, u32[]{:S(2)}) async-start(bf16[8,2,8192]{2,1,0:T(2,128)(2,1)} %all_to_all.31), calls=%async_computation.4 | async-start | bytes 524288 | tf_op jit(solution)/shard_map/all_to_all | solution.py:77
Sparse Core Ops, SparseCore 0:
  32.7 54.3 all-gather.1
  124.6 98.9 reduce-scatter.1

commit v5 on v3

--- a/solution.py
+++ b/solution.py
@@ -20,17 +20,10 @@
     slot_index = row_tag * CAP + slot_rank
     selector = jnp.arange(own_rows, dtype=jnp.int32)[:, None] == slot_index[None, :]
 
-    meta_col = lax.broadcasted_iota(jnp.int32, (local_rows, META), 1)
-    t = targets[:, None]
-    meta = jnp.where(
-        meta_col == 0,
-        (t >> 7).astype(jnp.float32),
-        jnp.where(
-            meta_col == 1,
-            (t & 127).astype(jnp.float32),
-            jnp.where(meta_col == 2, row_grad[:, None].astype(jnp.float32), 0.0),
-        ),
-    ).astype(jnp.bfloat16)
+    fields = jnp.stack(
+        [(targets >> 7).astype(jnp.bfloat16), (targets & 127).astype(jnp.bfloat16), row_grad], axis=1
+    )
+    meta = jnp.pad(fields, ((0, 0), (0, META - 3)))
     payload = jnp.concatenate([hidden_states, meta], axis=1)
     send = jnp.dot(
         selector.astype(jnp.bfloat16), payload, preferred_element_type=jnp.float32
@@ -72,11 +65,13 @@
     ).astype(jnp.bfloat16)
     back = jnp.concatenate([own_grad, back_meta], axis=1)
     returned = lax.all_to_all(back, "head", split_axis=0, concat_axis=0, tiled=True)
-    restored = jnp.dot(
-        selector.T.astype(jnp.bfloat16), returned, preferred_element_type=jnp.float32
-    ).astype(jnp.bfloat16)
-    hidden_grad = restored[:, :width]
-    row_loss = restored[:, width]
+    pick = selector.T.astype(jnp.bfloat16)
+    hidden_grad = jnp.dot(pick, returned[:, :width], preferred_element_type=jnp.float32).astype(
+        jnp.bfloat16
+    )
+    row_loss = jnp.dot(pick, returned[:, width:], preferred_element_type=jnp.float32)[:, 0].astype(
+        jnp.bfloat16
+    )
     return (row_loss, hidden_grad)
 
 

time: 251 us -> 251 us (level)
  no operation moved by 1% of the time
where the time goes in v5:
time: 251 us
  waiting for transfers between devices  160 us (64%)
  blocking collectives  37.7 us (15%)
  matrix products  23.7 us (9%)
  between operations  14.1 us (6%)
  other arithmetic  6.76 us (3%)
  starting transfers between devices  5.86 us (2%)
  local copies, waits for them, and re-layouts  2.7 us (1%)
    reduce_scatter x1, waiting for transfers between devices, per_device(): lax.psum_scatter(partial_value, 'vocab', scatter_dimension=0, tiled=True)  99 us
    all_gather x1, waiting for transfers between devices, per_device(): gathered = lax.all_gather(arrived, 'vocab', axis=0, tiled=True)  54.5 us
    all_to_all x1, blocking collectives, per_device(): lax.all_to_all(send, 'head', split_axis=0, concat_axis=0, tiled=True)  20.3 us
    all_to_all x1, blocking collectives, per_device(): lax.all_to_all(back, 'head', split_axis=0, concat_axis=0, tiled=True)  17.4 us
    dot_general x1, matrix products, per_device(): jnp.dot(gathered[:, :width], weight, preferred_element_type=jnp.float32)  11 us
    dot_general x1, matrix products, per_device(): lax.dot_general(dlogits, weight, (((1,), (1,)), ((), ())), preferred_elem...  10.5 us
    all_to_all x1, waiting for transfers between devices, per_device(): lax.all_to_all(copies, 'vocab', split_axis=0, concat_axis=0, tiled=True)  6.41 us
    all_to_all x1, starting transfers between devices, per_device(): lax.all_to_all(copies, 'vocab', split_axis=0, concat_axis=0, tiled=True)  5.78 us
  transfers between devices with their start and end apart: 3, of which 3 were waited for; matrix products, arithmetic and copies ran while one was open for 1% of the time, Pallas kernels for 0%

profile of v5, /device:TPU:2, one launch (start us, length us, event | category | flops | bytes accessed | tf_op | source)
XLA Modules:
  0.0 250.8 jit_solution(4007518822533623300)
XLA Ops:
  7.2 0.0 all-gather.2.cloned.1.call-start
  7.2 0.9 convert_reduce_fusion.1
  8.1 0.7 multiply_add_fusion
  8.8 0.7 convert_bitcast_fusion.1
  9.4 0.7 pad_maximum_fusion.2
  10.1 0.1 copy.21
  10.2 1.1 convolution_convert_fusion.1
  11.3 0.1 all_to_all.19
  11.4 20.3 %all_to_all.29 = bf16[8,2,8320]{2,1,0:T(2,128)(2,1)S(1)} all-to-all(bf16[8,2,8320]{2,1,0:T(2,128)(2,1)S(1)} %all_to_all.19), channel_id=1, replica_groups=mesh['head'=8,'vocab'=32] {'head'}, dimensions={0} | all-to-all | bytes 532480 | tf_op jit(solution)/shard_map/all_to_all | solution.py:32
  31.7 0.8 all_to_all.21
  32.6 0.0 all-gather.2.cloned.1.call-update
  32.6 54.5 %all-gather.2.cloned.1.call-done = bf16[512,8320]{1,0:T(8,128)(2,1)} async-done(((bf16[16,8320]{1,0:T(8,128)(2,1)}), bf16[512,8320]{1,0:T(8,128)(2,1)}) %all-gather.2.cloned.1.call-update) | async-done | bytes 8519696 | tf_op jit(solution)/shard_map/all_gather | solution.py:33
  87.2 1.2 add_reduce_fusion
  88.4 11.0 %fusion.34 = (f32[512]{0:T(512)S(1)}, f32[512,512]{0,1:T(8,128)S(1)}) fusion(bf16[1,8192,512]{2,1,0:T(8,128)(2,1)} %param.6, bf16[512,8320]{1,0:T(8,128)(2,1)} %all-gather.2.cloned.1.call-done), kind=kOutput, calls=%fused_computation.59 | convolution fusion | flops 4295228928 | bytes 17827840 | tf_op jit(solution)/shard_map/dot_general | solution.py:41
  99.4 0.3 exponential_reduce_fusion
  99.7 0.8 broadcast_in_dim.15
  100.4 5.8 %all-to-all-start.1 = ((f32[32,3,512]{2,1,0:T(4,128)}), f32[32,3,512]{2,1,0:T(4,128)S(1)}, u32[]{:S(2)}, u32[]{:S(2)}) async-start(f32[32,3,512]{2,1,0:T(4,128)} %broadcast_in_dim.15), calls=%async_computation.1 | async-start | bytes 524288 | tf_op jit(solution)/shard_map/all_to_all | solution.py:49
  106.2 0.0 reduce-scatter.2.cloned.1.call-start
  106.3 1.1 convert_reduce_fusion
  107.4 6.4 %all-to-all-done.1 = f32[32,3,512]{2,1,0:T(4,128)S(1)} async-done(((f32[32,3,512]{2,1,0:T(4,128)}), f32[32,3,512]{2,1,0:T(4,128)S(1)}, u32[]{:S(2)}, u32[]{:S(2)}) %all-to-all-start.1) | async-done | bytes 196640 | tf_op jit(solution)/shard_map/all_to_all | solution.py:49
  113.8 0.2 slice_reduce_fusion.2
  114.0 10.5 %convolution_convert_fusion = bf16[512,8192]{1,0:T(8,128)(2,1)} fusion(bf16[1,8192,512]{2,1,0:T(8,128)(2,1)} %param.6, f32[512,512]{0,1:T(8,128)S(1)} %get-tuple-element.11, f32[512]{0:T(512)S(1)} %fusion.25, f32[512]{0:T(512)S(1)} %get-tuple-element.4, s32[512]{0:T(512)S(1)} %add_reduce_fusion, f32[512]{0:T(512)S(1)} %convert_reduce_fusion, ...), kind=kOutput, calls=%fused_computation | convolution fusion | flops 4300996608 | bytes 17836032 | tf_op jit(solution)/shard_map/dot_general | solution.py:58
  124.5 0.0 reduce-scatter.2.cloned.1.call-update
  124.5 0.1 dynamic_slice.3
  124.6 0.1 select_convert_fusion
  124.7 99.0 %reduce-scatter.2.cloned.1.call-done = bf16[16,8192]{1,0:T(8,128)(2,1)} async-done(((bf16[512,8192]{1,0:T(8,128)(2,1)}), bf16[16,8192]{1,0:T(8,128)(2,1)}) %reduce-scatter.2.cloned.1.call-update) | async-done | bytes 262160 | tf_op jit(solution)/shard_map/reduce_scatter | solution.py:61
  223.6 1.0 pad_maximum_fusion
  224.6 0.1 all_to_all.23
  224.7 17.4 %all_to_all.30 = bf16[8,2,8320]{2,1,0:T(2,128)(2,1)S(1)} all-to-all(bf16[8,2,8320]{2,1,0:T(2,128)(2,1)S(1)} %all_to_all.23), channel_id=1, replica_groups=mesh['head'=8,'vocab'=32] {'head'}, dimensions={0} | all-to-all | bytes 532480 | tf_op jit(solution)/shard_map/all_to_all | solution.py:67
  242.1 0.1 all_to_all.25
  242.2 0.2 convolution_convert_fusion.3
  242.4 0.9 convolution_convert_fusion.2
  243.3 0.6 slice_reduce_fusion.1
  (5 shorter events, 0.1 us)
Async XLA Ops:
  7.2 80.0 %all-gather.2.cloned.1.call-start = ((), (), s32[]{:S(2)}) async-start(), calls=%async_computation.4 | async-start | bytes 8785920 | tf_op jit(solution)/shard_map/all_gather | solution.py:33
  100.4 13.4 %all-to-all-start.1 = ((f32[32,3,512]{2,1,0:T(4,128)}), f32[32,3,512]{2,1,0:T(4,128)S(1)}, u32[]{:S(2)}, u32[]{:S(2)}) async-start(f32[32,3,512]{2,1,0:T(4,128)} %broadcast_in_dim.15), calls=%async_computation.1 | async-start | bytes 524288 | tf_op jit(solution)/shard_map/all_to_all | solution.py:49
  106.2 117.4 %reduce-scatter.2.cloned.1.call-start = ((), (), s32[]{:S(2)}) async-start(), calls=%async_computation.5 | async-start | bytes 8650752 | tf_op jit(solution)/shard_map/reduce_scatter | solution.py:61
Sparse Core Ops, SparseCore 0:
  32.7 54.3 all-gather.1
  124.6 98.9 reduce-scatter.1
